TPU v7x, 512 devices: a whole 4x4x16 slice. The times are simulated.
512 devices in a mesh: row: 64 (over z, x), rep: 8 (over y, core).
Axes of the slice: x: 4, y: 4, z: 16, core: 2. Of those that a mesh axis runs over, the one named last changes fastest.
Arguments:
- features: bfloat16 [16384, 128], P('row', 'rep'), may hold values from -6 to 6
- owner_index: int32 [16384], P('row'), may hold values from 0 to 16383, as said below
- block_cols: int32 [128, 64], P('row', 'rep'), may hold values from 0 to 127, as said below
- block_count: int32 [128], P('row'), may hold values from 1 to 64, as said below
- tiles: bfloat16 [128, 64, 128, 128], P('row', 'rep'), may hold values from -0.109375 to 0.109375
- weight: bfloat16 [128, 256], P(None, 'rep'), may hold values from -0.75 to 0.75
- bias: float32 [256], P('rep'), may hold values from -4 to 4
- grad_out: bfloat16 [16384, 256], P('row', 'rep'), may hold values from -6 to 6
Outputs:
- hidden: bfloat16 [16384, 256], P('row', 'rep')
- weight_grad: float32 [128, 256], P(None, 'rep')
- bias_grad: float32 [256], P('rep')
Inputs may be any that keep to these rules, and one draw needn't show every extreme that they name: `owner_index`: A permutation; the 256 rows of each loader shard hold exactly 4 positions of every partition's 2*128 rows. `block_cols`: the block columns of one block row are distinct. Block column c belongs to partition c // 2. Over all slots of one partition's 2 block rows, exactly 1 distinct block columns of each partition are named. `block_count`: some block row has all 64 slots live.
All inputs are finite; a program needn't handle non-finite values.
Results may differ from a plain program's by a relative error of at most 0.017.
Values may be sent and summed in bfloat16 or wider, within the bound.
No kernel may reach another device: no remote copies, remote signals or barrier semaphores. Data moves between devices by JAX's collectives and lax.ppermute only.
A program may use at most 64 MiB of HBM per device.

v0:
```python
import jax
import jax.numpy as jnp
from jax import lax
from jax.sharding import PartitionSpec as P


def sum_over(x, axis_name, count):
    rows = x.shape[0]
    pieces = x.reshape((count, rows // count) + x.shape[1:])
    got = lax.all_to_all(pieces, axis_name, 0, 0, tiled=True)
    reduced = jnp.sum(got.astype(jnp.float32), axis=0)
    return reduced


def spread(x, axis_name, count):
    wide = jnp.broadcast_to(x[None], (count,) + x.shape)
    return lax.all_to_all(wide, axis_name, 0, 0, tiled=True)


def on_device(features, owner_index, block_cols, block_count, tiles, weight, bias, grad_out):
    rows_part, cols_dev = features.shape
    parts = lax.axis_size("row")
    reps = lax.axis_size("rep")
    per_pair = rows_part // parts
    rb, slots_dev, size_blk = (tiles.shape[0], tiles.shape[1], tiles.shape[2])
    destination = owner_index // rows_part
    order = jnp.argsort(destination, stable=True)
    send_rows = features[order]
    send_pos = (owner_index[order] % rows_part).astype(jnp.bfloat16)
    packet = jnp.concatenate([send_rows.T, send_pos[None, :]], axis=0)
    everyone = spread(packet, "row", parts)
    width = cols_dev + 1
    grouped = (
        everyone.reshape(parts, width, parts, per_pair)
        .transpose(2, 1, 0, 3)
        .reshape(parts, width, rows_part)
    )
    pos = grouped[:, cols_dev, :].astype(jnp.int32)
    values = grouped[:, :cols_dev, :]
    cols_all = lax.all_gather(block_cols, "rep", axis=1, tiled=True)
    part_of = cols_all // rb
    half_of = cols_all % rb
    part_ids = jnp.arange(parts, dtype=jnp.int32)
    hit = part_of[None, :, :] == part_ids[:, None, None]
    half = jnp.max(jnp.where(hit, half_of[None, :, :], 0), axis=(1, 2))
    node_ids = jnp.arange(size_blk, dtype=jnp.int32)
    target = half[:, None, None] * size_blk + node_ids[None, None, :]
    pick = (pos[:, :, None] == target).astype(jnp.bfloat16)
    needed = jnp.einsum("qfg,qgn->qfn", values, pick, preferred_element_type=jnp.float32).astype(
        jnp.bfloat16
    )
    peer_parts = part_of.reshape(rb, reps, slots_dev).transpose(1, 0, 2)
    outgoing = needed[peer_parts]
    incoming = lax.all_to_all(outgoing, "rep", 0, 0, tiled=True)
    slot_ids = lax.axis_index("rep") * slots_dev + jnp.arange(slots_dev, dtype=jnp.int32)
    live = slot_ids[None, :] < block_count[:, None]
    tiles_live = jnp.where(live[:, :, None, None], tiles, jnp.zeros_like(tiles))
    partial = jnp.einsum(
        "rsin,jrsfn->rijf", tiles_live, incoming, preferred_element_type=jnp.float32
    )
    partial = partial.reshape(rows_part, reps * cols_dev)
    agg_part = sum_over(partial, "rep", reps).astype(jnp.bfloat16)
    agg = spread(agg_part, "rep", reps).reshape(rows_part, reps * cols_dev)
    pre = jnp.dot(agg, weight, preferred_element_type=jnp.float32) + bias
    hidden = jax.nn.silu(pre).astype(jnp.bfloat16)
    sig = jax.nn.sigmoid(pre)
    dpre = (grad_out.astype(jnp.float32) * sig * (1.0 + pre * (1.0 - sig))).astype(jnp.bfloat16)
    weight_term = jnp.dot(agg.T, dpre, preferred_element_type=jnp.float32)
    bias_term = jnp.sum(dpre.astype(jnp.float32), axis=0)
    flat = jnp.concatenate([weight_term.reshape(-1), bias_term])
    lanes = 128
    chunk = lanes * -(-flat.shape[0] // (parts * lanes))
    flat = jnp.pad(flat, (0, parts * chunk - flat.shape[0])).reshape(parts, chunk)
    total = spread(sum_over(flat, "row", parts), "row", parts).reshape(-1)
    n_w = weight_term.size
    weight_grad = total[:n_w].reshape(weight_term.shape)
    bias_grad = total[n_w : n_w + bias_term.shape[0]]
    return (hidden, weight_grad, bias_grad)


def solution(mesh):
    placed = (
        P("row", "rep"),
        P("row"),
        P("row", "rep"),
        P("row"),
        P("row", "rep", None, None),
        P(None, "rep"),
        P("rep"),
        P("row", "rep"),
    )
    return jax.shard_map(
        on_device,
        mesh=mesh,
        in_specs=placed,
        out_specs=(P("row", "rep"), P(None, "rep"), P("rep")),
        check_vma=False,
    )
```

profile of v0, /device:TPU:8, one launch (start us, length us, event | category | flops | bytes accessed | tf_op | source)
XLA Modules:
  0.0 153.3 jit_solution(980085118121361113)
XLA Ops:
  0.6 0.0 copy-start
  0.6 0.7 and_select_fusion.3
  1.3 3.2 %sort.17 = (s32[256]{0:T(256)}, s32[256]{0:T(256)S(1)}) sort(s32[256]{0:T(256)S(1)} %and_select_fusion.3, s32[256]{0:T(256)S(1)} %iota.22), dimensions={0}, to_apply=%region_0.1 | sort | flops 2048 | bytes 4096 | tf_op jit(solution)/shard_map/jit(argsort)/sort | solution.py:27
  4.5 2.0 %gather_fusion.1 = s32[256]{0:T(256)S(1)} fusion(s32[256]{0:T(256)} %param.9, s32[1024]{0:T(1024)S(1)} %pad_clamp_fusion.1), kind=kCustom, calls=%fused_computation.1 | custom fusion | bytes 3072 | tf_op jit(solution)/shard_map/gather | solution.py:29
  6.5 0.8 copy.76
  7.3 0.9 gather_fusion
  8.2 0.1 copy.77
  8.3 0.0 copy-start.1
  8.3 0.9 broadcast_in_dim.35
  9.2 18.6 %all-to-all-start = ((bf16[64,17,256]{2,1,0:T(8,128)(2,1)}), bf16[64,17,256]{2,1,0:T(8,128)(2,1)S(1)}, u32[]{:S(2)}, u32[]{:S(2)}) async-start(bf16[64,17,256]{2,1,0:T(8,128)(2,1)} %broadcast_in_dim.35), calls=%async_computation | async-start | bytes 1572864 | tf_op jit(solution)/shard_map/all_to_all | solution.py:17
  27.8 0.0 copy-done.1
  27.8 8.8 %all-gather = s32[8,8,2]{1,2,0:T(2,128)S(1)} all-gather(s32[1,8,2]{1,2,0:T(2,128)S(1)} %bitcast.68), channel_id=1, replica_groups=mesh['row'=64,'rep'=8] {'rep'}, dimensions={0}, use_global_device_ids=true | all-gather | bytes 576 | tf_op jit(solution)/shard_map/all_gather | solution.py:40
  36.6 0.1 reshape.183
  36.7 0.1 reshape.148
  36.8 0.1 reshape.172
  36.9 0.1 select_reduce_fusion
  37.0 0.1 iota_add_fusion
  37.1 34.8 %all-to-all-done = bf16[64,17,256]{2,1,0:T(8,128)(2,1)S(1)} async-done(((bf16[64,17,256]{2,1,0:T(8,128)(2,1)}), bf16[64,17,256]{2,1,0:T(8,128)(2,1)S(1)}, u32[]{:S(2)}, u32[]{:S(2)}) %all-to-all-start) | async-done | bytes 557088 | tf_op jit(solution)/shard_map/all_to_all | solution.py:17
  71.8 0.8 copy.78
  72.7 1.7 %copy.79 = bf16[64,17,64,4]{0,3,2,1:T(4,128)(2,1)S(1)} copy(bf16[64,17,64,4]{2,3,0,1:T(4,128)(2,1)S(1)} %bitcast.60) | data formatting | bytes 1114112 | tf_op jit(solution)/shard_map/transpose | solution.py:35
  74.4 0.1 slice.23
  74.5 0.8 copy.96
  75.4 0.1 copy.81
  75.4 3.7 %fusion.4 = bf16[64,16,128]{2,1,0:T(8,128)(2,1)S(1)} fusion(bf16[64,16,256]{2,1,0:T(8,128)(2,1)S(1)} %copy.96, s32[64,128]{1,0:T(8,128)S(1)} %iota_add_fusion, s32[64,256]{1,0:T(8,128)S(1)} %copy.81), kind=kOutput, calls=%fused_computation.7 | convolution fusion | flops 69337088 | bytes 884736 | tf_op jit(solution)/shard_map/qfg,qgn->qfn/dot_general | solution.py:49
  79.1 0.0 copy-start.2
  79.1 1.5 gather_fusion.2
  80.6 4.9 %all-to-all-start.1 = ((bf16[8,2,8,16,128]{4,3,2,1,0:T(8,128)(2,1)}), bf16[8,2,8,16,128]{4,3,2,1,0:T(8,128)(2,1)S(1)}, u32[]{:S(2)}, u32[]{:S(2)}) async-start(bf16[8,2,8,16,128]{4,3,2,1,0:T(8,128)(2,1)} %bitcast.12), calls=%async_computation.1 | async-start | bytes 1048576 | tf_op jit(solution)/shard_map/all_to_all | solution.py:54
  85.5 0.0 copy-done.4
  85.6 0.1 broadcast_compare_fusion.1
  85.6 8.8 %all-to-all-done.1 = bf16[8,2,8,16,128]{4,3,2,1,0:T(8,128)(2,1)S(1)} async-done(((bf16[8,2,8,16,128]{4,3,2,1,0:T(8,128)(2,1)}), bf16[8,2,8,16,128]{4,3,2,1,0:T(8,128)(2,1)S(1)}, u32[]{:S(2)}, u32[]{:S(2)}) %all-to-all-start.1) | async-done | bytes 524320 | tf_op jit(solution)/shard_map/all_to_all | solution.py:54
  94.4 0.0 copy-done.2
  94.4 0.4 convolution_bitcast_fusion
  94.8 0.0 copy-start.3
  94.8 0.0 copy-start.5
  94.8 0.1 copy.85
  95.0 0.2 reshape_reshape.6
  95.2 0.2 copy.86
  95.4 8.5 %all_to_all.30 = f32[8,32,128]{2,1,0:T(8,128)S(1)} all-to-all(f32[8,32,128]{2,1,0:T(8,128)S(1)} %copy.86), channel_id=1, replica_groups=mesh['row'=64,'rep'=8] {'rep'}, dimensions={0} | all-to-all | bytes 262144 | tf_op jit(solution)/shard_map/all_to_all | solution.py:10
  103.9 8.0 %all_to_all.31 = bf16[8,32,128]{2,1,0:T(8,128)(2,1)S(1)} all-to-all(bf16[8,32,128]{2,1,0:T(8,128)(2,1)S(1)} %broadcast_in_dim.39), channel_id=1, replica_groups=mesh['row'=64,'rep'=8] {'rep'}, dimensions={0} | all-to-all | bytes 131072 | tf_op jit(solution)/shard_map/all_to_all | solution.py:17
  111.9 0.0 copy-done.5
  112.0 0.9 convert_reduce_fusion
  112.8 0.2 fusion.16
  113.0 0.1 reshape.150
  113.1 20.2 %all_to_all.32 = f32[64,1,128]{2,1,0:T(1,128)S(1)} all-to-all(f32[64,1,128]{2,1,0:T(1,128)S(1)} %bitcast.64), channel_id=1, replica_groups=mesh['row'=64,'rep'=8] {'row'}, dimensions={0} | all-to-all | bytes 65536 | tf_op jit(solution)/shard_map/all_to_all | solution.py:10
  133.4 18.6 %all_to_all.33 = f32[64,1,128]{2,1,0:T(1,128)S(1)} all-to-all(f32[64,1,128]{2,1,0:T(1,128)S(1)} %broadcast_in_dim.40), channel_id=1, replica_groups=mesh['row'=64,'rep'=8] {'row'}, dimensions={0} | all-to-all | bytes 65536 | tf_op jit(solution)/shard_map/all_to_all | solution.py:17
  152.0 0.5 slice.26
  152.5 0.1 reshape.151
  152.6 0.7 copy.91
  (22 shorter events, 0.2 us)
Async XLA Ops:
  0.6 111.3 %copy-start = (bf16[128,32]{0,1:T(8,128)(2,1)S(1)}, bf16[128,32]{0,1:T(8,128)(2,1)}, u32[]{:S(2)}) copy-start(bf16[128,32]{0,1:T(8,128)(2,1)} %param.13) | copy-start | bytes 24580
  8.3 19.5 %copy-start.1 = (s32[2,8]{1,0:T(2,128)S(1)}, s32[2,8]{1,0:T(2,128)}, u32[]{:S(2)}) copy-start(s32[2,8]{1,0:T(2,128)} %param.10) | copy-start | bytes 196
  9.2 62.6 %all-to-all-start = ((bf16[64,17,256]{2,1,0:T(8,128)(2,1)}), bf16[64,17,256]{2,1,0:T(8,128)(2,1)S(1)}, u32[]{:S(2)}, u32[]{:S(2)}) async-start(bf16[64,17,256]{2,1,0:T(8,128)(2,1)} %broadcast_in_dim.35), calls=%async_computation | async-start | bytes 1572864 | tf_op jit(solution)/shard_map/all_to_all | solution.py:17
  79.1 6.4 %copy-start.4 = (s32[2]{0:T(128)S(1)}, s32[2]{0:T(128)}, u32[]{:S(2)}) copy-start(s32[2]{0:T(128)} %param.11) | copy-start | bytes 28
  79.1 15.3 %copy-start.2 = (bf16[2,8,128,128]{3,2,1,0:T(8,128)(2,1)S(1)}, bf16[2,8,128,128]{3,2,1,0:T(8,128)(2,1)}, u32[]{:S(2)}) copy-start(bf16[2,8,128,128]{3,2,1,0:T(8,128)(2,1)} %param.12) | copy-start | bytes 1572868
  80.6 13.8 %all-to-all-start.1 = ((bf16[8,2,8,16,128]{4,3,2,1,0:T(8,128)(2,1)}), bf16[8,2,8,16,128]{4,3,2,1,0:T(8,128)(2,1)S(1)}, u32[]{:S(2)}, u32[]{:S(2)}) async-start(bf16[8,2,8,16,128]{4,3,2,1,0:T(8,128)(2,1)} %bitcast.12), calls=%async_computation.1 | async-start | bytes 1048576 | tf_op jit(solution)/shard_map/all_to_all | solution.py:54
  94.8 17.1 %copy-start.3 = (bf16[256,32]{0,1:T(8,128)(2,1)S(1)}, bf16[256,32]{0,1:T(8,128)(2,1)}, u32[]{:S(2)}) copy-start(bf16[256,32]{0,1:T(8,128)(2,1)} %param.15) | copy-start | bytes 49156
  94.8 17.1 %copy-start.5 = (f32[32]{0:T(128)S(1)}, f32[32]{0:T(128)}, u32[]{:S(2)}) copy-start(f32[32]{0:T(128)} %param.14) | copy-start | bytes 388
where the time goes:
time: 154 us; the launch traced here: 153 us
  blocking collectives  64.1 us (42%)
  waiting for transfers between devices  43.6 us (28%)
  starting transfers between devices  23.5 us (15%)
  local copies, waits for them, and re-layouts  11.9 us (8%)
  matrix products  5.13 us (3%)
  other arithmetic  4.26 us (3%)
    all_to_all x1, waiting for transfers between devices, spread(): return lax.all_to_all(wide, axis_name, 0, 0, tiled=True)  34.8 us
    all_to_all x2, blocking collectives, sum_over(): got = lax.all_to_all(pieces, axis_name, 0, 0, tiled=True)  28.8 us
    all_to_all x2, blocking collectives, spread(): return lax.all_to_all(wide, axis_name, 0, 0, tiled=True)  26.5 us
    all_to_all x1, starting transfers between devices, spread(): return lax.all_to_all(wide, axis_name, 0, 0, tiled=True)  18.6 us
    all_to_all x1, waiting for transfers between devices, on_device(): incoming = lax.all_to_all(outgoing, 'rep', 0, 0, tiled=True)  8.81 us
    all_gather x1, blocking collectives, on_device(): cols_all = lax.all_gather(block_cols, 'rep', axis=1, tiled=True)  8.77 us
    all_to_all x1, starting transfers between devices, on_device(): incoming = lax.all_to_all(outgoing, 'rep', 0, 0, tiled=True)  4.92 us
    dot_general x1, matrix products, on_device(): jnp.einsum('qfg,qgn->qfn', values, pick, preferred_element_type=jnp.float32)  3.69 us
  transfers between devices with their start and end apart: 2, of which 2 were waited for; matrix products, arithmetic and copies ran while one was open for 0% of the time, Pallas kernels for 0%

commit v1 on v0

--- a/solution.py
+++ b/solution.py
@@ -37,7 +37,9 @@
     )
     pos = grouped[:, cols_dev, :].astype(jnp.int32)
     values = grouped[:, :cols_dev, :]
-    cols_all = lax.all_gather(block_cols, "rep", axis=1, tiled=True)
+    cols_all = jnp.concatenate(
+        lax.all_to_all(jnp.stack([block_cols] * lax.axis_size("rep")), "rep", 0, 0), axis=1
+    )
     part_of = cols_all // rb
     half_of = cols_all % rb
     part_ids = jnp.arange(parts, dtype=jnp.int32)

time: 154 us -> 160 us (1.039)
  waiting for transfers between devices: 43.6 us -> 52.7 us
  blocking collectives: 64.1 us -> 55.3 us
  starting transfers between devices: 23.5 us -> 28.3 us
    all_to_all x1, waiting for transfers between devices: 34.8 us -> 43.9 us  [spread(): return lax.all_to_all(wide, axis_name, 0, 0, tiled=True)]
    all_to_all x0 -> x1, starting transfers between devices: none -> 9.07 us  [on_device(): lax.all_to_all(jnp.stack([block_cols] * lax.axis_size('rep')), 'rep', 0, 0)]
    all_gather x1 -> x0, blocking collectives: 8.77 us -> none  [on_device(): cols_all = lax.all_gather(block_cols, 'rep', axis=1, tiled=True)]
    all_to_all x1, starting transfers between devices: 18.6 us -> 14.4 us  [spread(): return lax.all_to_all(wide, axis_name, 0, 0, tiled=True)]
  transfers between devices with their start and end apart: 2 -> 3, of which waited for: 2 -> 2; matrix products, arithmetic and copies ran while one was open for 0% -> 5% of each run, Pallas kernels for 0% -> 0%
where the time goes in v1:
time: 160 us
  blocking collectives  55.3 us (35%)
  waiting for transfers between devices  52.7 us (33%)
  starting transfers between devices  28.3 us (18%)
  local copies, waits for them, and re-layouts  13.1 us (8%)
  matrix products  5.13 us (3%)
  other arithmetic  4.27 us (3%)
    all_to_all x1, waiting for transfers between devices, spread(): return lax.all_to_all(wide, axis_name, 0, 0, tiled=True)  43.9 us
    all_to_all x2, blocking collectives, sum_over(): got = lax.all_to_all(pieces, axis_name, 0, 0, tiled=True)  28.8 us
    all_to_all x2, blocking collectives, spread(): return lax.all_to_all(wide, axis_name, 0, 0, tiled=True)  26.5 us
    all_to_all x1, starting transfers between devices, spread(): return lax.all_to_all(wide, axis_name, 0, 0, tiled=True)  14.4 us
    all_to_all x1, starting transfers between devices, on_device(): lax.all_to_all(jnp.stack([block_cols] * lax.axis_size('rep')), 'rep', 0, 0)  9.07 us
    all_to_all x1, waiting for transfers between devices, on_device(): incoming = lax.all_to_all(outgoing, 'rep', 0, 0, tiled=True)  8.81 us
    all_to_all x1, starting transfers between devices, on_device(): incoming = lax.all_to_all(outgoing, 'rep', 0, 0, tiled=True)  4.8 us
    dot_general x1, matrix products, on_device(): jnp.einsum('qfg,qgn->qfn', values, pick, preferred_element_type=jnp.float32)  3.69 us
  transfers between devices with their start and end apart: 3, of which 2 were waited for; matrix products, arithmetic and copies ran while one was open for 5% of the time, Pallas kernels for 0%

profile of v1, /device:TPU:8, one launch (start us, length us, event | category | flops | bytes accessed | tf_op | source)
XLA Modules:
  0.0 159.7 jit_solution(6043022150055757966)
XLA Ops:
  0.6 0.0 copy-start
  0.6 1.3 stack.2
  1.9 9.1 %all-to-all-start.1 = ((s32[8,2,8]{2,1,0:T(2,128)}), s32[8,2,8]{2,1,0:T(2,128)S(1)}, u32[]{:S(2)}, u32[]{:S(2)}) async-start(s32[8,2,8]{2,1,0:T(2,128)} %stack.2), calls=%async_computation.1 | async-start | bytes 16384 | tf_op jit(solution)/shard_map/all_to_all | solution.py:41
  11.0 0.7 and_select_fusion.4
  11.7 3.2 %sort.17 = (s32[256]{0:T(256)}, s32[256]{0:T(256)S(1)}) sort(s32[256]{0:T(256)S(1)} %and_select_fusion.4, s32[256]{0:T(256)S(1)} %iota.22), dimensions={0}, to_apply=%region_0.1 | sort | flops 2048 | bytes 4096 | tf_op jit(solution)/shard_map/jit(argsort)/sort | solution.py:27
  14.9 2.0 %gather_fusion.1 = s32[256]{0:T(256)S(1)} fusion(s32[256]{0:T(256)} %param.9, s32[1024]{0:T(1024)S(1)} %pad_clamp_fusion.1), kind=kCustom, calls=%fused_computation.1 | custom fusion | bytes 3072 | tf_op jit(solution)/shard_map/gather | solution.py:29
  16.9 0.8 copy.71
  17.7 0.9 gather_fusion
  18.5 0.1 copy.72
  18.6 0.0 all-to-all-done.1
  18.6 0.9 broadcast_in_dim.35
  19.6 14.4 %all-to-all-start = ((bf16[64,17,256]{2,1,0:T(8,128)(2,1)}), bf16[64,17,256]{2,1,0:T(8,128)(2,1)S(1)}, u32[]{:S(2)}, u32[]{:S(2)}) async-start(bf16[64,17,256]{2,1,0:T(8,128)(2,1)} %broadcast_in_dim.35), calls=%async_computation | async-start | bytes 1572864 | tf_op jit(solution)/shard_map/all_to_all | solution.py:17
  34.0 0.1 reshape.202
  34.1 0.1 reshape.226
  34.2 0.1 select_reduce_fusion
  34.4 0.1 iota_add_fusion
  34.4 43.9 %all-to-all-done = bf16[64,17,256]{2,1,0:T(8,128)(2,1)S(1)} async-done(((bf16[64,17,256]{2,1,0:T(8,128)(2,1)}), bf16[64,17,256]{2,1,0:T(8,128)(2,1)S(1)}, u32[]{:S(2)}, u32[]{:S(2)}) %all-to-all-start) | async-done | bytes 557088 | tf_op jit(solution)/shard_map/all_to_all | solution.py:17
  78.4 0.8 copy.73
  79.2 1.7 %copy.74 = bf16[64,17,64,4]{0,3,2,1:T(4,128)(2,1)S(1)} copy(bf16[64,17,64,4]{2,3,0,1:T(4,128)(2,1)S(1)} %bitcast.34) | data formatting | bytes 1114112 | tf_op jit(solution)/shard_map/transpose | solution.py:35
  80.9 0.1 slice.23
  81.0 0.8 copy.90
  81.9 0.1 copy.76
  82.0 3.7 %fusion.4 = bf16[64,16,128]{2,1,0:T(8,128)(2,1)S(1)} fusion(bf16[64,16,256]{2,1,0:T(8,128)(2,1)S(1)} %copy.90, s32[64,128]{1,0:T(8,128)S(1)} %iota_add_fusion, s32[64,256]{1,0:T(8,128)S(1)} %copy.76), kind=kOutput, calls=%fused_computation.7 | convolution fusion | flops 69337088 | bytes 884736 | tf_op jit(solution)/shard_map/qfg,qgn->qfn/dot_general | solution.py:51
  85.6 0.0 copy-start.1
  85.7 1.5 gather_fusion.2
  87.1 4.8 %all-to-all-start.2 = ((bf16[8,2,8,16,128]{4,3,2,1,0:T(8,128)(2,1)}), bf16[8,2,8,16,128]{4,3,2,1,0:T(8,128)(2,1)S(1)}, u32[]{:S(2)}, u32[]{:S(2)}) async-start(bf16[8,2,8,16,128]{4,3,2,1,0:T(8,128)(2,1)} %bitcast.9), calls=%async_computation.2 | async-start | bytes 1048576 | tf_op jit(solution)/shard_map/all_to_all | solution.py:56
  91.9 0.0 copy-done.3
  91.9 0.1 broadcast_compare_fusion.2
  92.0 8.8 %all-to-all-done.2 = bf16[8,2,8,16,128]{4,3,2,1,0:T(8,128)(2,1)S(1)} async-done(((bf16[8,2,8,16,128]{4,3,2,1,0:T(8,128)(2,1)}), bf16[8,2,8,16,128]{4,3,2,1,0:T(8,128)(2,1)S(1)}, u32[]{:S(2)}, u32[]{:S(2)}) %all-to-all-start.2) | async-done | bytes 524320 | tf_op jit(solution)/shard_map/all_to_all | solution.py:56
  100.8 0.0 copy-done.1
  100.8 0.4 convolution_bitcast_fusion
  101.2 0.0 copy-start.2
  101.2 0.0 copy-start.4
  101.2 0.1 copy.79
  101.3 0.2 reshape_reshape.6
  101.6 0.2 copy.80
  101.8 8.5 %all_to_all.35 = f32[8,32,128]{2,1,0:T(8,128)S(1)} all-to-all(f32[8,32,128]{2,1,0:T(8,128)S(1)} %copy.80), channel_id=1, replica_groups=mesh['row'=64,'rep'=8] {'rep'}, dimensions={0} | all-to-all | bytes 262144 | tf_op jit(solution)/shard_map/all_to_all | solution.py:10
  110.3 8.0 %all_to_all.36 = bf16[8,32,128]{2,1,0:T(8,128)(2,1)S(1)} all-to-all(bf16[8,32,128]{2,1,0:T(8,128)(2,1)S(1)} %broadcast_in_dim.39), channel_id=1, replica_groups=mesh['row'=64,'rep'=8] {'rep'}, dimensions={0} | all-to-all | bytes 131072 | tf_op jit(solution)/shard_map/all_to_all | solution.py:17
  118.3 0.0 copy-done
  118.3 0.0 copy-done.2
  118.4 0.9 convert_reduce_fusion
  119.2 0.2 fusion.16
  119.4 0.1 reshape.204
  119.5 20.2 %all_to_all.37 = f32[64,1,128]{2,1,0:T(1,128)S(1)} all-to-all(f32[64,1,128]{2,1,0:T(1,128)S(1)} %bitcast.38), channel_id=1, replica_groups=mesh['row'=64,'rep'=8] {'row'}, dimensions={0} | all-to-all | bytes 65536 | tf_op jit(solution)/shard_map/all_to_all | solution.py:10
  139.8 18.6 %all_to_all.38 = f32[64,1,128]{2,1,0:T(1,128)S(1)} all-to-all(f32[64,1,128]{2,1,0:T(1,128)S(1)} %broadcast_in_dim.40), channel_id=1, replica_groups=mesh['row'=64,'rep'=8] {'row'}, dimensions={0} | all-to-all | bytes 65536 | tf_op jit(solution)/shard_map/all_to_all | solution.py:17
  158.4 0.5 slice.26
  158.9 0.1 reshape.205
  159.0 0.7 copy.85
  (20 shorter events, 0.2 us)
Async XLA Ops:
  0.6 117.7 %copy-start = (bf16[128,32]{0,1:T(8,128)(2,1)S(1)}, bf16[128,32]{0,1:T(8,128)(2,1)}, u32[]{:S(2)}) copy-start(bf16[128,32]{0,1:T(8,128)(2,1)} %param.13) | copy-start | bytes 24580
  1.9 16.7 %all-to-all-start.1 = ((s32[8,2,8]{2,1,0:T(2,128)}), s32[8,2,8]{2,1,0:T(2,128)S(1)}, u32[]{:S(2)}, u32[]{:S(2)}) async-start(s32[8,2,8]{2,1,0:T(2,128)} %stack.2), calls=%async_computation.1 | async-start | bytes 16384 | tf_op jit(solution)/shard_map/all_to_all | solution.py:41
  19.6 58.8 %all-to-all-start = ((bf16[64,17,256]{2,1,0:T(8,128)(2,1)}), bf16[64,17,256]{2,1,0:T(8,128)(2,1)S(1)}, u32[]{:S(2)}, u32[]{:S(2)}) async-start(bf16[64,17,256]{2,1,0:T(8,128)(2,1)} %broadcast_in_dim.35), calls=%async_computation | async-start | bytes 1572864 | tf_op jit(solution)/shard_map/all_to_all | solution.py:17
  85.6 6.3 %copy-start.3 = (s32[2]{0:T(128)S(1)}, s32[2]{0:T(128)}, u32[]{:S(2)}) copy-start(s32[2]{0:T(128)} %param.11) | copy-start | bytes 28
  85.6 15.2 %copy-start.1 = (bf16[2,8,128,128]{3,2,1,0:T(8,128)(2,1)S(1)}, bf16[2,8,128,128]{3,2,1,0:T(8,128)(2,1)}, u32[]{:S(2)}) copy-start(bf16[2,8,128,128]{3,2,1,0:T(8,128)(2,1)} %param.12) | copy-start | bytes 1572868
  87.1 13.7 %all-to-all-start.2 = ((bf16[8,2,8,16,128]{4,3,2,1,0:T(8,128)(2,1)}), bf16[8,2,8,16,128]{4,3,2,1,0:T(8,128)(2,1)S(1)}, u32[]{:S(2)}, u32[]{:S(2)}) async-start(bf16[8,2,8,16,128]{4,3,2,1,0:T(8,128)(2,1)} %bitcast.9), calls=%async_computation.2 | async-start | bytes 1048576 | tf_op jit(solution)/shard_map/all_to_all | solution.py:56
  101.2 17.1 %copy-start.2 = (bf16[256,32]{0,1:T(8,128)(2,1)S(1)}, bf16[256,32]{0,1:T(8,128)(2,1)}, u32[]{:S(2)}) copy-start(bf16[256,32]{0,1:T(8,128)(2,1)} %param.15) | copy-start | bytes 49156
  101.2 17.1 %copy-start.4 = (f32[32]{0:T(128)S(1)}, f32[32]{0:T(128)}, u32[]{:S(2)}) copy-start(f32[32]{0:T(128)} %param.14) | copy-start | bytes 388
